TPU v7x, 32 devices: a whole 2x2x4 slice. The times are simulated.
32 devices in a mesh: grid: 8 (over z, y), band: 4 (over x, core).
Axes of the slice: x: 2, y: 2, z: 4, core: 2. Of those that a mesh axis runs over, the one named last changes fastest.
Arguments:
- orbitals: float32 [2048, 512], P('grid', 'band'), may hold values from -30 to 30
- potential: float32 [2048], P('grid'), may hold values from -1 to 1
- fitted: bfloat16 [512, 2048], P('band', 'grid'), may hold values from -6 to 6
- points: int32 [512], P('grid'), may hold values from -1 to 255, as said below
Outputs:
- updated: float32 [2048, 512], P('grid', 'band')
Inputs may be any that keep to these rules, and one draw needn't show every extreme that they name: Each block of 64 slots of one index of grid holds distinct grid points in its first slots and -1 in the rest; the numbers of filled slots of blocks 2i and 2i + 1 sum to 64, so that 256 slots are filled in all, and some block is full.
All inputs are finite; a program needn't handle non-finite values.
Results may differ from a plain program's by a relative error of at most 0.024.
Values may be sent and summed in bfloat16 or wider, within the bound.
No kernel may reach another device: no remote copies, remote signals or barrier semaphores. Data moves between devices by JAX's collectives and lax.ppermute only.
A program may use at most 64 MiB of HBM per device.

v0:
```python
import jax
import jax.numpy as jnp
from jax import lax
from jax.sharding import PartitionSpec as P

ITERS = 2


def body(orbitals, potential, fitted, points):
    rows = orbitals.shape[0]
    block_width = orbitals.shape[1]
    nbands = lax.axis_size("band")
    ngroups = lax.axis_size("grid")
    total_orbitals = block_width * nbands
    valid_mask = points >= 0
    safe_idx = jnp.where(valid_mask, points, 0)
    psi = orbitals
    for step in range(ITERS):
        orbital_block = psi.astype(jnp.bfloat16)
        selected_points = jnp.where(
            valid_mask[:, None], orbital_block[safe_idx], jnp.zeros((), jnp.bfloat16)
        )
        collocation_matrix = lax.all_gather(selected_points, "grid", axis=0, tiled=True)
        product = lax.dot_general(
            collocation_matrix,
            orbital_block,
            (((1,), (1,)), ((), ())),
            preferred_element_type=jnp.float32,
        )
        proj = lax.psum_scatter(
            (product / total_orbitals).astype(jnp.bfloat16), "band", scatter_dimension=0, tiled=True
        ).astype(jnp.float32)
        tile_blocks = (fitted.astype(jnp.float32) * proj).astype(jnp.bfloat16)
        orbitals_at_slots = lax.all_to_all(
            collocation_matrix, "band", split_axis=0, concat_axis=1, tiled=True
        )
        partial_value = lax.dot_general(
            tile_blocks,
            orbitals_at_slots,
            (((0,), (0,)), ((), ())),
            preferred_element_type=jnp.float32,
        )
        applied = lax.psum_scatter(
            partial_value.astype(jnp.bfloat16), "band", scatter_dimension=1, tiled=True
        ).astype(jnp.float32)
        fresh = psi - 0.25 * (potential[:, None] * psi - applied)
        squares = lax.psum(jnp.sum(fresh * fresh, axis=0), "grid")
        psi = fresh * lax.rsqrt(squares / (rows * ngroups) + 1e-06)
    return psi


def solution(mesh):
    in_specs = (P("grid", "band"), P("grid"), P("band", "grid"), P("grid"))
    out_specs = P("grid", "band")
    return jax.shard_map(body, mesh=mesh, in_specs=in_specs, out_specs=out_specs, check_vma=False)
```

profile of v0, /device:TPU:0, one launch (start us, length us, event | category | flops | bytes accessed | tf_op | source)
XLA Modules:
  0.0 209.6 jit_solution(11900437040815080563)
XLA Ops:
  6.5 0.0 copy-start.3
  6.5 0.0 reduce-scatter.9.cloned.1.call-start
  6.5 0.7 compare_select_fusion
  7.3 0.0 copy-done.3
  7.3 0.9 convert_element_type.41
  8.2 0.6 gather_fusion
  8.8 0.1 broadcast_select_fusion.1
  8.9 32.3 %all_gather.6 = bf16[512,128]{1,0:T(8,128)(2,1)S(1)} all-gather(bf16[64,128]{1,0:T(8,128)(2,1)S(1)} %broadcast_select_fusion.1), channel_id=1, replica_groups=mesh['grid'=8,'band'=4] {'grid'}, dimensions={0}, use_global_device_ids=true | all-gather | bytes 147456 | tf_op jit(solution)/shard_map/all_gather | solution.py:23
  41.2 0.9 fusion
  42.1 0.0 reduce-scatter.9.cloned.1.call-update
  42.2 0.0 reduce-scatter.13.cloned.1.call-start
  42.2 0.1 copy.7
  42.4 0.0 copy-start.1
  42.4 7.3 %all_to_all.38 = bf16[4,128,128]{1,2,0:T(8,128)(2,1)S(1)} all-to-all(bf16[4,128,128]{1,2,0:T(8,128)(2,1)S(1)} %copy.7), channel_id=1, replica_groups=mesh['grid'=8,'band'=4] {'band'}, dimensions={0} | all-to-all | bytes 262144 | tf_op jit(solution)/shard_map/all_to_all | solution.py:34
  49.7 13.6 %reduce-scatter.9.cloned.1.call-done = bf16[128,256]{1,0:T(8,128)(2,1)} async-done(((bf16[512,256]{1,0:T(8,128)(2,1)}), bf16[128,256]{1,0:T(8,128)(2,1)}) %reduce-scatter.9.cloned.1.call-update) | async-done | bytes 65552 | tf_op jit(solution)/shard_map/reduce_scatter | solution.py:30
  63.3 0.0 copy-done.1
  63.3 1.1 convolution_convert_fusion.1
  64.4 0.8 copy.9
  65.2 0.0 reduce-scatter.13.cloned.1.call-update
  65.2 0.0 copy-start
  65.3 0.0 reduce-scatter.11.cloned.1.call-start
  65.3 20.6 %reduce-scatter.13.cloned.1.call-done = bf16[128,256]{1,0:T(8,128)(2,1)} async-done(((bf16[512,256]{1,0:T(8,128)(2,1)}), bf16[128,256]{1,0:T(8,128)(2,1)}) %reduce-scatter.13.cloned.1.call-update) | async-done | bytes 65552
  85.9 0.0 copy-start.2
  85.9 1.0 copy.10
  86.9 0.0 copy-done
  86.9 0.0 copy-done.2
  86.9 0.1 multiply_reduce_fusion.1
  87.0 21.4 %psum.14 = f32[128]{0:T(128)S(1)} all-reduce(f32[128]{0:T(128)S(1)} %multiply_reduce_fusion.1), channel_id=1, replica_groups=mesh['grid'=8,'band'=4] {'grid'}, use_global_device_ids=true, to_apply=%region_3.4 | all-reduce | flops 128 | bytes 1024 | tf_op jit(solution)/shard_map/psum | solution.py:47
  108.4 0.1 multiply_convert_fusion
  108.5 0.6 gather_fusion.1
  109.2 0.1 broadcast_select_fusion
  109.3 30.5 %all_gather.7 = bf16[512,128]{1,0:T(8,128)(2,1)S(1)} all-gather(bf16[64,128]{1,0:T(8,128)(2,1)S(1)} %broadcast_select_fusion), channel_id=1, replica_groups=mesh['grid'=8,'band'=4] {'grid'}, dimensions={0}, use_global_device_ids=true | all-gather | bytes 147456 | tf_op jit(solution)/shard_map/all_gather | solution.py:23
  139.8 0.9 fusion.1
  140.7 0.0 reduce-scatter.11.cloned.1.call-update
  140.7 0.0 reduce-scatter.15.cloned.1.call-start
  140.8 0.1 copy.8
  140.9 7.0 %all_to_all.39 = bf16[4,128,128]{1,2,0:T(8,128)(2,1)S(1)} all-to-all(bf16[4,128,128]{1,2,0:T(8,128)(2,1)S(1)} %copy.8), channel_id=1, replica_groups=mesh['grid'=8,'band'=4] {'band'}, dimensions={0} | all-to-all | bytes 262144 | tf_op jit(solution)/shard_map/all_to_all | solution.py:34
  147.9 9.3 %reduce-scatter.11.cloned.1.call-done = bf16[128,256]{1,0:T(8,128)(2,1)} async-done(((bf16[512,256]{1,0:T(8,128)(2,1)}), bf16[128,256]{1,0:T(8,128)(2,1)}) %reduce-scatter.11.cloned.1.call-update) | async-done | bytes 65552 | tf_op jit(solution)/shard_map/reduce_scatter | solution.py:30
  157.3 1.1 convolution_convert_fusion
  158.3 0.8 copy.11
  159.2 0.0 reduce-scatter.15.cloned.1.call-update
  159.2 20.6 %reduce-scatter.15.cloned.1.call-done = bf16[128,256]{1,0:T(8,128)(2,1)} async-done(((bf16[512,256]{1,0:T(8,128)(2,1)}), bf16[128,256]{1,0:T(8,128)(2,1)}) %reduce-scatter.15.cloned.1.call-update) | async-done | bytes 65552
  179.8 0.9 copy.12
  180.7 0.1 multiply_reduce_fusion
  180.9 21.4 %psum.15 = f32[128]{0:T(128)S(1)} all-reduce(f32[128]{0:T(128)S(1)} %multiply_reduce_fusion), channel_id=1, replica_groups=mesh['grid'=8,'band'=4] {'grid'}, use_global_device_ids=true, to_apply=%region_7.8 | all-reduce | flops 128 | bytes 1024 | tf_op jit(solution)/shard_map/psum | solution.py:47
  202.3 0.8 broadcast_multiply_fusion
  (4 shorter events, 0.0 us)
Async XLA Ops:
  6.5 0.7 copy-start.3
  6.5 56.7 %reduce-scatter.9.cloned.1.call-start = ((), (), s32[]{:S(2)}) async-start(), calls=%async_computation.6 | async-start | bytes 327680 | tf_op jit(solution)/shard_map/reduce_scatter | solution.py:30
  42.2 43.8 %reduce-scatter.13.cloned.1.call-start = ((), (), s32[]{:S(2)}) async-start(), calls=%async_computation.8 | async-start | bytes 327680
  42.4 20.9 %copy-start.1 = (bf16[128,256]{1,0:T(8,128)(2,1)S(1)}, bf16[128,256]{1,0:T(8,128)(2,1)}, u32[]{:S(2)}) copy-start(bf16[128,256]{1,0:T(8,128)(2,1)} %param.6) | copy-start | bytes 196612
  65.2 21.7 %copy-start = (f32[256,128]{1,0:T(8,128)S(1)}, f32[256,128]{1,0:T(8,128)}, u32[]{:S(2)}) copy-start(f32[256,128]{1,0:T(8,128)} %param.4) | copy-start | bytes 393220
  65.3 92.0 %reduce-scatter.11.cloned.1.call-start = ((), (), s32[]{:S(2)}) async-start(), calls=%async_computation.7 | async-start | bytes 327680 | tf_op jit(solution)/shard_map/reduce_scatter | solution.py:30
  85.9 1.0 copy-start.2
  140.7 39.1 %reduce-scatter.15.cloned.1.call-start = ((), (), s32[]{:S(2)}) async-start(), calls=%async_computation.9 | async-start | bytes 327680
Sparse Core Ops, SparseCore 0:
  42.3 20.9 reduce-scatter.8
  65.9 19.9 reduce-scatter.12
  140.8 16.3 reduce-scatter.10
  159.7 20.0 reduce-scatter.14
where the time goes:
time: 210 us
  blocking collectives  120 us (57%)
  waiting for transfers between devices  64.2 us (31%)
  between operations  13.2 us (6%)
  local copies, waits for them, and re-layouts  5.13 us (2%)
  matrix products  4.03 us (2%)
  other arithmetic  2.98 us (1%)
    all_gather x2, blocking collectives, body(): lax.all_gather(selected_points, 'grid', axis=0, tiled=True)  62.8 us
    psum x2, blocking collectives, body(): squares = lax.psum(jnp.sum(fresh * fresh, axis=0), 'grid')  42.8 us
    unnamed x6, waiting for transfers between devices  41.3 us
    reduce_scatter x2, waiting for transfers between devices, body(): lax.psum_scatter((product / total_orbitals).astype(jnp.bfloat16), 'band',...  22.9 us
    all_to_all x2, blocking collectives, body(): lax.all_to_all(collocation_matrix, 'band', split_axis=0, concat_axis=1, t...  14.3 us
  transfers between devices with their start and end apart: 4, of which 4 were waited for; matrix products, arithmetic and copies ran while one was open for 0% of the time, Pallas kernels for 0%

commit v1 on v0

--- a/solution.py
+++ b/solution.py
@@ -4,6 +4,32 @@
 from jax.sharding import PartitionSpec as P
 
 ITERS = 2
+
+
+def number_the_streams(inputs, a_name, join_dim):
+    oldest = lax.axis_size(a_name)
+    x_next = lax.axis_index(a_name)
+    carry_in, arr_next, block_out = (oldest, x_next, inputs.shape[join_dim])
+    pieces_in = [(q, (q + 1) % carry_in) for q in range(carry_in)]
+    t_next = jnp.zeros(
+        (*inputs.shape[:join_dim], carry_in * block_out, *inputs.shape[join_dim + 1 :]),
+        inputs.dtype,
+    )
+    by_place = [(q, (q - 1) % carry_in) for q in range(carry_in)]
+    long_array = kept_arr = inputs
+    t_next = lax.dynamic_update_slice_in_dim(t_next, inputs, arr_next * block_out, axis=join_dim)
+    vec_out = carry_in // 2
+    for b in tuple(range(1, vec_out + 1)):
+        long_array = lax.ppermute(long_array, a_name, pieces_in)
+        t_next = lax.dynamic_update_slice_in_dim(
+            t_next, long_array, (arr_next - b) % carry_in * block_out, axis=join_dim
+        )
+        if b < carry_in - vec_out:
+            kept_arr = lax.ppermute(kept_arr, a_name, by_place)
+            t_next = lax.dynamic_update_slice_in_dim(
+                t_next, kept_arr, (arr_next + b) % carry_in * block_out, axis=join_dim
+            )
+    return t_next
 
 
 def body(orbitals, potential, fitted, points):
@@ -20,7 +46,7 @@
         selected_points = jnp.where(
             valid_mask[:, None], orbital_block[safe_idx], jnp.zeros((), jnp.bfloat16)
         )
-        collocation_matrix = lax.all_gather(selected_points, "grid", axis=0, tiled=True)
+        collocation_matrix = number_the_streams(selected_points, "grid", 0)
         product = lax.dot_general(
             collocation_matrix,
             orbital_block,

time: 210 us -> 197 us (0.938)
  blocking collectives: 120 us -> 57.1 us
  starting transfers between devices: 0.13 us -> 30.2 us
  waiting for transfers between devices: 64.2 us -> 83.4 us
    all_gather x2 -> x0, blocking collectives: 62.8 us -> none  [body(): lax.all_gather(selected_points, 'grid', axis=0, tiled=True)]
    ppermute x0 -> x14, starting transfers between devices: none -> 30.1 us  [the longest x6 27 us: number_the_streams(): kept_arr = lax.ppermute(kept_arr, a_name, by_place)]
    ppermute x0 -> x14, waiting for transfers between devices: none -> 22.7 us  [the longest x8 22.7 us: number_the_streams(): long_array = lax.ppermute(long_array, a_name, pieces_in)]
    reduce_scatter x2, waiting for transfers between devices: 22.9 us -> 19.4 us  [body(): lax.psum_scatter((product / total_orbitals).astype(jnp.bfloat16), 'band',...]
  transfers between devices with their start and end apart: 4 -> 18, of which waited for: 4 -> 12; matrix products, arithmetic and copies ran while one was open for 0% -> 0% of each run, Pallas kernels for 0% -> 0%
where the time goes in v1:
time: 197 us; the launch traced here: 196 us
  waiting for transfers between devices  83.4 us (42%)
  blocking collectives  57.1 us (29%)
  starting transfers between devices  30.2 us (15%)
  between operations  13.3 us (7%)
  local copies, waits for them, and re-layouts  5.94 us (3%)
  matrix products  4.01 us (2%)
  other arithmetic  2.29 us (1%)
    psum x2, blocking collectives, body(): squares = lax.psum(jnp.sum(fresh * fresh, axis=0), 'grid')  42.7 us
    unnamed x6, waiting for transfers between devices  41.3 us
    ppermute x6, starting transfers between devices, number_the_streams(): kept_arr = lax.ppermute(kept_arr, a_name, by_place)  27 us
    ppermute x8, waiting for transfers between devices, number_the_streams(): long_array = lax.ppermute(long_array, a_name, pieces_in)  22.7 us
    reduce_scatter x2, waiting for transfers between devices, body(): lax.psum_scatter((product / total_orbitals).astype(jnp.bfloat16), 'band',...  19.4 us
    all_to_all x2, blocking collectives, body(): lax.all_to_all(collocation_matrix, 'band', split_axis=0, concat_axis=1, t...  14.4 us
    unnamed x12, local copies, waits for them, and re-layouts  4.24 us
  transfers between devices with their start and end apart: 18, of which 12 were waited for; matrix products, arithmetic and copies ran while one was open for 0% of the time, Pallas kernels for 0%

profile of v1, /device:TPU:0, one launch (start us, length us, event | category | flops | bytes accessed | tf_op | source)
XLA Modules:
  0.0 196.2 jit_solution(9249835438079931413)
XLA Ops:
  6.5 0.7 copy-done.3
  7.2 0.9 convert_element_type.41
  8.1 0.6 gather_fusion
  8.8 0.1 constant_dynamic-update-slice_fusion.15
  8.9 3.0 %collective-permute-start = (bf16[64,128]{1,0:T(8,128)(2,1)S(1)}, bf16[64,128]{1,0:T(8,128)(2,1)S(1)}, u32[]{:S(2)}, u32[]{:S(2)}) collective-permute-start(bf16[64,128]{1,0:T(8,128)(2,1)S(1)} %get-tuple-element.8), channel_id=1, source_target_pairs={{0,4},{4,8},{8,12},{12,16},{16,20},{20,24},{24,28},{28,0},{1,5},{5... | collective-permute-start | bytes 49160 | tf_op jit(solution)/shard_map/ppermute | solution.py:23
  11.9 3.1 %collective-permute-start.1 = (bf16[64,128]{1,0:T(8,128)(2,1)S(1)}, bf16[64,128]{1,0:T(8,128)(2,1)S(1)}, u32[]{:S(2)}, u32[]{:S(2)}) collective-permute-start(bf16[64,128]{1,0:T(8,128)(2,1)S(1)} %get-tuple-element.8), channel_id=1, source_target_pairs={{0,28},{4,0},{8,4},{12,8},{16,12},{20,16},{24,20},{28,24},{1,29},{... | collective-permute-start | bytes 49160 | tf_op jit(solution)/shard_map/ppermute | solution.py:28
  15.0 1.7 collective-permute-done
  16.7 0.0 collective-permute-start.2
  16.7 0.0 collective-permute-done.1
  16.7 4.8 %collective-permute-start.3 = (bf16[64,128]{1,0:T(8,128)(2,1)S(1)}, bf16[64,128]{1,0:T(8,128)(2,1)S(1)}, u32[]{:S(2)}, u32[]{:S(2)}) collective-permute-start(bf16[64,128]{1,0:T(8,128)(2,1)S(1)} %collective-permute-done.1), channel_id=1, source_target_pairs={{0,28},{4,0},{8,4},{12,8},{16,12},{20,16},{24,20},{28,24},{1,29},{... | collective-permute-start | bytes 49160 | tf_op jit(solution)/shard_map/ppermute | solution.py:28
  21.5 1.6 collective-permute-done.2
  23.1 0.0 collective-permute-start.4
  23.1 0.0 collective-permute-done.3
  23.1 4.8 %collective-permute-start.5 = (bf16[64,128]{1,0:T(8,128)(2,1)S(1)}, bf16[64,128]{1,0:T(8,128)(2,1)S(1)}, u32[]{:S(2)}, u32[]{:S(2)}) collective-permute-start(bf16[64,128]{1,0:T(8,128)(2,1)S(1)} %collective-permute-done.3), channel_id=1, source_target_pairs={{0,28},{4,0},{8,4},{12,8},{16,12},{20,16},{24,20},{28,24},{1,29},{... | collective-permute-start | bytes 49160 | tf_op jit(solution)/shard_map/ppermute | solution.py:28
  27.9 1.6 collective-permute-done.4
  29.5 0.0 collective-permute-start.6
  29.5 0.0 collective-permute-done.5
  29.6 6.4 %collective-permute-done.6 = bf16[64,128]{1,0:T(8,128)(2,1)S(1)} collective-permute-done((bf16[64,128]{1,0:T(8,128)(2,1)S(1)}, bf16[64,128]{1,0:T(8,128)(2,1)S(1)}, u32[]{:S(2)}, u32[]{:S(2)}) %collective-permute-start.6) | collective-permute-done | bytes 16416 | tf_op jit(solution)/shard_map/ppermute | solution.py:23
  36.0 0.9 fusion
  36.9 0.0 reduce-scatter.9.cloned.1.call-update
  36.9 0.0 reduce-scatter.13.cloned.1.call-start
  37.0 7.3 %all_to_all.38 = bf16[4,128,128]{2,1,0:T(8,128)(2,1)S(1)} all-to-all(bf16[4,128,128]{2,1,0:T(8,128)(2,1)S(1)} %bitcast.17), channel_id=1, replica_groups=mesh['grid'=8,'band'=4] {'band'}, dimensions={0} | all-to-all | bytes 262144 | tf_op jit(solution)/shard_map/all_to_all | solution.py:60
  44.3 0.1 copy.7
  44.5 10.1 %reduce-scatter.9.cloned.1.call-done = bf16[128,256]{1,0:T(8,128)(2,1)} async-done(((bf16[512,256]{1,0:T(8,128)(2,1)}), bf16[128,256]{1,0:T(8,128)(2,1)}) %reduce-scatter.9.cloned.1.call-update) | async-done | bytes 65552 | tf_op jit(solution)/shard_map/reduce_scatter | solution.py:56
  54.6 1.1 convolution_convert_fusion.1
  55.6 0.8 copy.9
  56.5 0.0 reduce-scatter.13.cloned.1.call-update
  56.5 0.0 copy-start
  56.5 0.0 reduce-scatter.11.cloned.1.call-start
  56.6 20.7 %reduce-scatter.13.cloned.1.call-done = bf16[128,256]{1,0:T(8,128)(2,1)} async-done(((bf16[512,256]{1,0:T(8,128)(2,1)}), bf16[128,256]{1,0:T(8,128)(2,1)}) %reduce-scatter.13.cloned.1.call-update) | async-done | bytes 65552
  77.2 1.0 copy.10
  78.2 0.1 multiply_reduce_fusion.1
  78.3 21.4 %psum.14 = f32[128]{0:T(128)S(1)} all-reduce(f32[128]{0:T(128)S(1)} %multiply_reduce_fusion.1), channel_id=1, replica_groups=mesh['grid'=8,'band'=4] {'grid'}, use_global_device_ids=true, to_apply=%region_3.4 | all-reduce | flops 128 | bytes 1024 | tf_op jit(solution)/shard_map/psum | solution.py:73
  99.7 0.1 multiply_convert_fusion
  99.8 0.6 gather_fusion.1
  100.5 0.1 constant_dynamic-update-slice_fusion.7
  100.6 0.1 collective-permute-start.7
  100.6 4.7 %collective-permute-start.8 = (bf16[64,128]{1,0:T(8,128)(2,1)S(1)}, bf16[64,128]{1,0:T(8,128)(2,1)S(1)}, u32[]{:S(2)}, u32[]{:S(2)}) collective-permute-start(bf16[64,128]{1,0:T(8,128)(2,1)S(1)} %get-tuple-element.6), channel_id=1, source_target_pairs={{0,28},{4,0},{8,4},{12,8},{16,12},{20,16},{24,20},{28,24},{1,29},{... | collective-permute-start | bytes 49160 | tf_op jit(solution)/shard_map/ppermute | solution.py:28
  105.3 1.7 collective-permute-done.7
  107.1 0.0 collective-permute-start.9
  107.1 0.0 collective-permute-done.8
  107.1 4.8 %collective-permute-start.10 = (bf16[64,128]{1,0:T(8,128)(2,1)S(1)}, bf16[64,128]{1,0:T(8,128)(2,1)S(1)}, u32[]{:S(2)}, u32[]{:S(2)}) collective-permute-start(bf16[64,128]{1,0:T(8,128)(2,1)S(1)} %collective-permute-done.8), channel_id=1, source_target_pairs={{0,28},{4,0},{8,4},{12,8},{16,12},{20,16},{24,20},{28,24},{1,29},{... | collective-permute-start | bytes 49160 | tf_op jit(solution)/shard_map/ppermute | solution.py:28
  111.9 1.6 collective-permute-done.9
  113.5 0.0 collective-permute-start.11
  113.5 0.0 collective-permute-done.10
  113.5 4.8 %collective-permute-start.12 = (bf16[64,128]{1,0:T(8,128)(2,1)S(1)}, bf16[64,128]{1,0:T(8,128)(2,1)S(1)}, u32[]{:S(2)}, u32[]{:S(2)}) collective-permute-start(bf16[64,128]{1,0:T(8,128)(2,1)S(1)} %collective-permute-done.10), channel_id=1, source_target_pairs={{0,28},{4,0},{8,4},{12,8},{16,12},{20,16},{24,20},{28,24},{1,29},{... | collective-permute-start | bytes 49160 | tf_op jit(solution)/shard_map/ppermute | solution.py:28
  118.3 1.6 collective-permute-done.11
  119.9 0.0 collective-permute-start.13
  119.9 0.0 collective-permute-done.12
  120.0 6.4 %collective-permute-done.13 = bf16[64,128]{1,0:T(8,128)(2,1)S(1)} collective-permute-done((bf16[64,128]{1,0:T(8,128)(2,1)S(1)}, bf16[64,128]{1,0:T(8,128)(2,1)S(1)}, u32[]{:S(2)}, u32[]{:S(2)}) %collective-permute-start.13) | collective-permute-done | bytes 16416 | tf_op jit(solution)/shard_map/ppermute | solution.py:23
  126.4 0.9 fusion.1
  127.3 0.0 reduce-scatter.11.cloned.1.call-update
  127.3 0.0 reduce-scatter.15.cloned.1.call-start
  127.4 7.0 %all_to_all.39 = bf16[4,128,128]{2,1,0:T(8,128)(2,1)S(1)} all-to-all(bf16[4,128,128]{2,1,0:T(8,128)(2,1)S(1)} %bitcast.16), channel_id=1, replica_groups=mesh['grid'=8,'band'=4] {'band'}, dimensions={0} | all-to-all | bytes 262144 | tf_op jit(solution)/shard_map/all_to_all | solution.py:60
  134.4 0.1 copy.8
  134.5 9.3 %reduce-scatter.11.cloned.1.call-done = bf16[128,256]{1,0:T(8,128)(2,1)} async-done(((bf16[512,256]{1,0:T(8,128)(2,1)}), bf16[128,256]{1,0:T(8,128)(2,1)}) %reduce-scatter.11.cloned.1.call-update) | async-done | bytes 65552 | tf_op jit(solution)/shard_map/reduce_scatter | solution.py:56
  143.8 1.1 convolution_convert_fusion
  144.9 0.8 copy.11
  145.8 0.0 reduce-scatter.15.cloned.1.call-update
  145.8 20.6 %reduce-scatter.15.cloned.1.call-done = bf16[128,256]{1,0:T(8,128)(2,1)} async-done(((bf16[512,256]{1,0:T(8,128)(2,1)}), bf16[128,256]{1,0:T(8,128)(2,1)}) %reduce-scatter.15.cloned.1.call-update) | async-done | bytes 65552
  166.4 0.9 copy.12
  167.3 0.1 multiply_reduce_fusion
  167.5 21.3 %psum.15 = f32[128]{0:T(128)S(1)} all-reduce(f32[128]{0:T(128)S(1)} %multiply_reduce_fusion), channel_id=1, replica_groups=mesh['grid'=8,'band'=4] {'grid'}, use_global_device_ids=true, to_apply=%region_7.8 | all-reduce | flops 128 | bytes 1024 | tf_op jit(solution)/shard_map/psum | solution.py:73
  188.8 0.8 broadcast_multiply_fusion
  (28 shorter events, 0.2 us)
Async XLA Ops:
  6.5 0.7 copy-start.3
  6.5 48.0 %reduce-scatter.9.cloned.1.call-start = ((), (), s32[]{:S(2)}) async-start(), calls=%async_computation.6 | async-start | bytes 327680 | tf_op jit(solution)/shard_map/reduce_scatter | solution.py:56
  8.9 7.8 %collective-permute-start = (bf16[64,128]{1,0:T(8,128)(2,1)S(1)}, bf16[64,128]{1,0:T(8,128)(2,1)S(1)}, u32[]{:S(2)}, u32[]{:S(2)}) collective-permute-start(bf16[64,128]{1,0:T(8,128)(2,1)S(1)} %get-tuple-element.8), channel_id=1, source_target_pairs={{0,4},{4,8},{8,12},{12,16},{16,20},{20,24},{24,28},{28,0},{1,5},{5... | collective-permute-start | bytes 49160 | tf_op jit(solution)/shard_map/ppermute | solution.py:23
  11.9 4.8 %collective-permute-start.1 = (bf16[64,128]{1,0:T(8,128)(2,1)S(1)}, bf16[64,128]{1,0:T(8,128)(2,1)S(1)}, u32[]{:S(2)}, u32[]{:S(2)}) collective-permute-start(bf16[64,128]{1,0:T(8,128)(2,1)S(1)} %get-tuple-element.8), channel_id=1, source_target_pairs={{0,28},{4,0},{8,4},{12,8},{16,12},{20,16},{24,20},{28,24},{1,29},{... | collective-permute-start | bytes 49160 | tf_op jit(solution)/shard_map/ppermute | solution.py:28
  16.7 6.4 %collective-permute-start.2 = (bf16[64,128]{1,0:T(8,128)(2,1)S(1)}, bf16[64,128]{1,0:T(8,128)(2,1)S(1)}, u32[]{:S(2)}, u32[]{:S(2)}) collective-permute-start(bf16[64,128]{1,0:T(8,128)(2,1)S(1)} %collective-permute-done), channel_id=1, source_target_pairs={{0,4},{4,8},{8,12},{12,16},{16,20},{20,24},{24,28},{28,0},{1,5},{5... | collective-permute-start | bytes 49160 | tf_op jit(solution)/shard_map/ppermute | solution.py:23
  16.7 6.4 %collective-permute-start.3 = (bf16[64,128]{1,0:T(8,128)(2,1)S(1)}, bf16[64,128]{1,0:T(8,128)(2,1)S(1)}, u32[]{:S(2)}, u32[]{:S(2)}) collective-permute-start(bf16[64,128]{1,0:T(8,128)(2,1)S(1)} %collective-permute-done.1), channel_id=1, source_target_pairs={{0,28},{4,0},{8,4},{12,8},{16,12},{20,16},{24,20},{28,24},{1,29},{... | collective-permute-start | bytes 49160 | tf_op jit(solution)/shard_map/ppermute | solution.py:28
  23.1 6.4 %collective-permute-start.4 = (bf16[64,128]{1,0:T(8,128)(2,1)S(1)}, bf16[64,128]{1,0:T(8,128)(2,1)S(1)}, u32[]{:S(2)}, u32[]{:S(2)}) collective-permute-start(bf16[64,128]{1,0:T(8,128)(2,1)S(1)} %collective-permute-done.2), channel_id=1, source_target_pairs={{0,4},{4,8},{8,12},{12,16},{16,20},{20,24},{24,28},{28,0},{1,5},{5... | collective-permute-start | bytes 49160 | tf_op jit(solution)/shard_map/ppermute | solution.py:23
  23.1 6.4 %collective-permute-start.5 = (bf16[64,128]{1,0:T(8,128)(2,1)S(1)}, bf16[64,128]{1,0:T(8,128)(2,1)S(1)}, u32[]{:S(2)}, u32[]{:S(2)}) collective-permute-start(bf16[64,128]{1,0:T(8,128)(2,1)S(1)} %collective-permute-done.3), channel_id=1, source_target_pairs={{0,28},{4,0},{8,4},{12,8},{16,12},{20,16},{24,20},{28,24},{1,29},{... | collective-permute-start | bytes 49160 | tf_op jit(solution)/shard_map/ppermute | solution.py:28
  29.5 6.4 %collective-permute-start.6 = (bf16[64,128]{1,0:T(8,128)(2,1)S(1)}, bf16[64,128]{1,0:T(8,128)(2,1)S(1)}, u32[]{:S(2)}, u32[]{:S(2)}) collective-permute-start(bf16[64,128]{1,0:T(8,128)(2,1)S(1)} %collective-permute-done.4), channel_id=1, source_target_pairs={{0,4},{4,8},{8,12},{12,16},{16,20},{20,24},{24,28},{28,0},{1,5},{5... | collective-permute-start | bytes 49160 | tf_op jit(solution)/shard_map/ppermute | solution.py:23
  36.9 40.3 %reduce-scatter.13.cloned.1.call-start = ((), (), s32[]{:S(2)}) async-start(), calls=%async_computation.8 | async-start | bytes 327680
  44.3 10.2 %copy-start.1 = (bf16[128,256]{1,0:T(8,128)(2,1)S(1)}, bf16[128,256]{1,0:T(8,128)(2,1)}, u32[]{:S(2)}) copy-start(bf16[128,256]{1,0:T(8,128)(2,1)} %param.6) | copy-start | bytes 196612
  56.5 21.7 %copy-start = (f32[256,128]{1,0:T(8,128)S(1)}, f32[256,128]{1,0:T(8,128)}, u32[]{:S(2)}) copy-start(f32[256,128]{1,0:T(8,128)} %param.4) | copy-start | bytes 393220
  56.5 87.3 %reduce-scatter.11.cloned.1.call-start = ((), (), s32[]{:S(2)}) async-start(), calls=%async_computation.7 | async-start | bytes 327680 | tf_op jit(solution)/shard_map/reduce_scatter | solution.py:56
  77.2 1.0 copy-start.2
  100.6 6.5 %collective-permute-start.7 = (bf16[64,128]{1,0:T(8,128)(2,1)S(1)}, bf16[64,128]{1,0:T(8,128)(2,1)S(1)}, u32[]{:S(2)}, u32[]{:S(2)}) collective-permute-start(bf16[64,128]{1,0:T(8,128)(2,1)S(1)} %get-tuple-element.6), channel_id=1, source_target_pairs={{0,4},{4,8},{8,12},{12,16},{16,20},{20,24},{24,28},{28,0},{1,5},{5... | collective-permute-start | bytes 49160 | tf_op jit(solution)/shard_map/ppermute | solution.py:23
  100.6 6.4 %collective-permute-start.8 = (bf16[64,128]{1,0:T(8,128)(2,1)S(1)}, bf16[64,128]{1,0:T(8,128)(2,1)S(1)}, u32[]{:S(2)}, u32[]{:S(2)}) collective-permute-start(bf16[64,128]{1,0:T(8,128)(2,1)S(1)} %get-tuple-element.6), channel_id=1, source_target_pairs={{0,28},{4,0},{8,4},{12,8},{16,12},{20,16},{24,20},{28,24},{1,29},{... | collective-permute-start | bytes 49160 | tf_op jit(solution)/shard_map/ppermute | solution.py:28
  107.1 6.4 %collective-permute-start.9 = (bf16[64,128]{1,0:T(8,128)(2,1)S(1)}, bf16[64,128]{1,0:T(8,128)(2,1)S(1)}, u32[]{:S(2)}, u32[]{:S(2)}) collective-permute-start(bf16[64,128]{1,0:T(8,128)(2,1)S(1)} %collective-permute-done.7), channel_id=1, source_target_pairs={{0,4},{4,8},{8,12},{12,16},{16,20},{20,24},{24,28},{28,0},{1,5},{5... | collective-permute-start | bytes 49160 | tf_op jit(solution)/shard_map/ppermute | solution.py:23
  107.1 6.4 %collective-permute-start.10 = (bf16[64,128]{1,0:T(8,128)(2,1)S(1)}, bf16[64,128]{1,0:T(8,128)(2,1)S(1)}, u32[]{:S(2)}, u32[]{:S(2)}) collective-permute-start(bf16[64,128]{1,0:T(8,128)(2,1)S(1)} %collective-permute-done.8), channel_id=1, source_target_pairs={{0,28},{4,0},{8,4},{12,8},{16,12},{20,16},{24,20},{28,24},{1,29},{... | collective-permute-start | bytes 49160 | tf_op jit(solution)/shard_map/ppermute | solution.py:28
  113.5 6.4 %collective-permute-start.11 = (bf16[64,128]{1,0:T(8,128)(2,1)S(1)}, bf16[64,128]{1,0:T(8,128)(2,1)S(1)}, u32[]{:S(2)}, u32[]{:S(2)}) collective-permute-start(bf16[64,128]{1,0:T(8,128)(2,1)S(1)} %collective-permute-done.9), channel_id=1, source_target_pairs={{0,4},{4,8},{8,12},{12,16},{16,20},{20,24},{24,28},{28,0},{1,5},{5... | collective-permute-start | bytes 49160 | tf_op jit(solution)/shard_map/ppermute | solution.py:23
  113.5 6.4 %collective-permute-start.12 = (bf16[64,128]{1,0:T(8,128)(2,1)S(1)}, bf16[64,128]{1,0:T(8,128)(2,1)S(1)}, u32[]{:S(2)}, u32[]{:S(2)}) collective-permute-start(bf16[64,128]{1,0:T(8,128)(2,1)S(1)} %collective-permute-done.10), channel_id=1, source_target_pairs={{0,28},{4,0},{8,4},{12,8},{16,12},{20,16},{24,20},{28,24},{1,29},{... | collective-permute-start | bytes 49160 | tf_op jit(solution)/shard_map/ppermute | solution.py:28
  119.9 6.4 %collective-permute-start.13 = (bf16[64,128]{1,0:T(8,128)(2,1)S(1)}, bf16[64,128]{1,0:T(8,128)(2,1)S(1)}, u32[]{:S(2)}, u32[]{:S(2)}) collective-permute-start(bf16[64,128]{1,0:T(8,128)(2,1)S(1)} %collective-permute-done.11), channel_id=1, source_target_pairs={{0,4},{4,8},{8,12},{12,16},{16,20},{20,24},{24,28},{28,0},{1,5},{5... | collective-permute-start | bytes 49160 | tf_op jit(solution)/shard_map/ppermute | solution.py:23
  127.3 39.1 %reduce-scatter.15.cloned.1.call-start = ((), (), s32[]{:S(2)}) async-start(), calls=%async_computation.9 | async-start | bytes 327680
Sparse Core Ops, SparseCore 0:
  37.0 17.4 reduce-scatter.8
  57.1 20.0 reduce-scatter.12
  127.4 16.3 reduce-scatter.10
  146.3 20.0 reduce-scatter.14
